TPU v7x, 256 devices: a whole 4x4x8 slice. The times are simulated.
256 devices in a mesh: dp: 8 (over x, z_hi), ctx: 32 (over z_lo, y, core).
Axes of the slice: x: 4, y: 4, z: 8 (z_hi: 2, z_lo: 4; z = z_hi * 4 + z_lo), core: 2. Of those that a mesh axis runs over, the one named last changes fastest.
Arguments:
- queries: bfloat16 [32768, 1024], P(('dp', 'ctx')), parts along dimension 0, may hold values from -8 to 8
- keys: bfloat16 [32768, 1024], P(('dp', 'ctx')), parts along dimension 0, may hold values from -8 to 8
- values: bfloat16 [32768, 1024], P(('dp', 'ctx')), parts along dimension 0, may hold values from -6 to 6
- grad_out: bfloat16 [32768, 1024], P(('dp', 'ctx')), parts along dimension 0, may hold values from -6 to 6
- rand_blocks: int32 [512, 3], P(('dp', 'ctx')), parts along dimension 0, may hold values from 0 to 1
- global_ids: int32 [16], P('dp'), parts along dimension 0, may hold values from 0 to 63
Outputs:
- attended: bfloat16 [32768, 1024], P(('dp', 'ctx')), parts along dimension 0
- grad_queries: bfloat16 [32768, 1024], P(('dp', 'ctx')), parts along dimension 0
- grad_keys: bfloat16 [32768, 1024], P(('dp', 'ctx')), parts along dimension 0
- grad_values: bfloat16 [32768, 1024], P(('dp', 'ctx')), parts along dimension 0
There are 8 independent parts, one for each index of `dp`. A program takes and returns all parts, laid end to end along the dimension named above; each array names one. Nothing has to cross between parts.
All inputs are finite; a program needn't handle non-finite values.
Results may differ from a plain program's by a relative error of at most 0.02.
Values may be sent and summed in bfloat16 or wider, within the bound.
No kernel may reach another device: no remote copies, remote signals or barrier semaphores. Data moves between devices by JAX's collectives and lax.ppermute only.
A program may use at most 128 MiB of HBM per device.

v0:
```python
import jax
import jax.numpy as jnp
from jax import lax
from jax.sharding import PartitionSpec as P

HEADS = 16
HEAD_DIM = 64
BLOCK = 64
RAND = 3
GLOBALS = 2
SCORE_FLOOR = -1e30


def padded_2(array, sides, width):
    for axis, dim in sides:
        size, length = (lax.axis_size(axis), array.shape[dim])
        up = [(i, (i + 1) % size) for i in range(size - 1)]
        down = [(j, i) for i, j in up]
        last = lax.slice_in_dim(array, length - width, length, axis=dim)
        first = lax.slice_in_dim(array, 0, width, axis=dim)
        before = lax.ppermute(last, axis, up)
        after = lax.ppermute(first, axis, down)
        array = jnp.concatenate([before, array, after], axis=dim)
    return array


def from_root(block, axis, source):
    block = jnp.where(lax.axis_index(axis) == source, block, jnp.zeros_like(block))
    return lax.psum(block, axis)


def partner_2(array, axis, distance):
    return lax.ppermute(array, axis, [(i, i ^ 1 << distance) for i in range(lax.axis_size(axis))])


def passed_along(array, axis, by):
    size = lax.axis_size(axis)
    pairs = [(i, i + by) for i in range(size) if 0 <= i + by < size]
    return lax.ppermute(array, axis, pairs)


def attend_blocks(query_blocks, key_blocks, value_blocks, grad_blocks, key_valid):
    scale_factor = HEAD_DIM ** (-0.5)
    scores = (
        jnp.einsum("jqhd,jkhd->jhqk", query_blocks, key_blocks, preferred_element_type=jnp.float32)
        * scale_factor
    )
    scores = jnp.where(key_valid[:, None, None, :], scores, SCORE_FLOOR)
    highest = jnp.max(scores, axis=-1, keepdims=True)
    raw_weights = jnp.exp(scores - highest)
    weight_total = jnp.sum(raw_weights, axis=-1, keepdims=True)
    probs = raw_weights / weight_total
    probs_low = probs.astype(jnp.bfloat16)
    attended = jnp.einsum(
        "jhqk,jkhd->jqhd", probs_low, value_blocks, preferred_element_type=jnp.float32
    )
    grad_probs = jnp.einsum(
        "jqhd,jkhd->jhqk", grad_blocks, value_blocks, preferred_element_type=jnp.float32
    )
    inner = jnp.sum(probs * grad_probs, axis=-1, keepdims=True)
    grad_scores = (scale_factor * probs * (grad_probs - inner)).astype(jnp.bfloat16)
    grad_query = jnp.einsum(
        "jhqk,jkhd->jqhd", grad_scores, key_blocks, preferred_element_type=jnp.float32
    )
    grad_key = jnp.einsum(
        "jhqk,jqhd->jkhd", grad_scores, query_blocks, preferred_element_type=jnp.float32
    )
    grad_value = jnp.einsum(
        "jhqk,jqhd->jkhd", probs_low, grad_blocks, preferred_element_type=jnp.float32
    )
    return (attended, grad_query, grad_key, grad_value, (highest, weight_total, inner))


def local(queries, keys, values, grad_out, rand_blocks, global_ids):
    tok_rows, width = queries.shape
    block_count = tok_rows // BLOCK
    listed = 3 + GLOBALS + RAND
    ctx_count = lax.axis_size("ctx")
    position = lax.axis_index("ctx")
    top_bit = ctx_count.bit_length() - 1
    block_iota = jnp.arange(block_count, dtype=jnp.int32)
    stacked = jnp.stack([keys, values])
    padded = padded_2(stacked, (("ctx", 1),), BLOCK)
    framed = padded.reshape(2, block_count + 2, BLOCK, width)
    window = jnp.concatenate([framed[:, :-2], framed[:, 1:-1], framed[:, 2:]], axis=2)
    owners = global_ids // block_count
    local_ids = global_ids % block_count
    own_pieces = jnp.stack(
        [
            lax.dynamic_slice_in_dim(stacked, local_ids[global_slot] * BLOCK, BLOCK, 1)
            for global_slot in range(GLOBALS)
        ],
        axis=1,
    )
    fetched = jnp.stack(
        [
            from_root(own_pieces[:, global_slot], "ctx", owners[global_slot])
            for global_slot in range(GLOBALS)
        ],
        axis=1,
    )
    global_part = jnp.broadcast_to(
        fetched.reshape(2, 1, GLOBALS * BLOCK, width), (2, block_count, GLOBALS * BLOCK, width)
    )
    pickers = []
    random_parts = []
    for matching in range(RAND):
        spread_bit = top_bit - 1 - matching
        picker = (rand_blocks[:, matching][:, None] == block_iota[None, :]).astype(jnp.bfloat16)
        partner = partner_2(stacked, "ctx", spread_bit).reshape(2, block_count, BLOCK, width)
        chosen = jnp.einsum(
            "jb,sbqd->sjqd", picker, partner, preferred_element_type=jnp.float32
        ).astype(jnp.bfloat16)
        pickers.append(picker)
        random_parts.append(chosen)
    every_key = jnp.concatenate([window, global_part] + random_parts, axis=2)
    key_blocks = every_key[0].reshape(block_count, listed * BLOCK, HEADS, HEAD_DIM)
    value_blocks = every_key[1].reshape(block_count, listed * BLOCK, HEADS, HEAD_DIM)
    global_block = position * block_count + block_iota
    seq_blocks = block_count * ctx_count
    left_ok = global_block > 0
    right_ok = global_block < seq_blocks - 1
    key_valid = jnp.concatenate(
        [
            jnp.broadcast_to(left_ok[:, None], (block_count, BLOCK)),
            jnp.ones((block_count, BLOCK), dtype=bool),
            jnp.broadcast_to(right_ok[:, None], (block_count, BLOCK)),
            jnp.ones((block_count, (GLOBALS + RAND) * BLOCK), dtype=bool),
        ],
        axis=1,
    )
    query_blocks = queries.reshape(block_count, BLOCK, HEADS, HEAD_DIM)
    grad_blocks = grad_out.reshape(block_count, BLOCK, HEADS, HEAD_DIM)
    attended, grad_query, grad_key, grad_value, softmax_stats = attend_blocks(
        query_blocks, key_blocks, value_blocks, grad_blocks, key_valid
    )
    split = jnp.stack([grad_key, grad_value]).reshape(2, block_count, listed, BLOCK, width)
    own_window = (
        jnp.pad(split[:, :, 0], ((0, 0), (0, 2), (0, 0), (0, 0)))
        + jnp.pad(split[:, :, 1], ((0, 0), (1, 1), (0, 0), (0, 0)))
        + jnp.pad(split[:, :, 2], ((0, 0), (2, 0), (0, 0), (0, 0)))
    )
    from_right = passed_along(own_window[:, 0], "ctx", -1)
    from_left = passed_along(own_window[:, -1], "ctx", 1)
    own_total = own_window[:, 1:-1]
    own_total = own_total.at[:, -1].add(from_right)
    own_total = own_total.at[:, 0].add(from_left)
    for matching in range(RAND):
        spread_bit = top_bit - 1 - matching
        terms = split[:, :, 3 + GLOBALS + matching]
        routed = jnp.einsum(
            "jb,sjqd->sbqd",
            pickers[matching].astype(jnp.float32),
            terms,
            precision=lax.Precision.HIGHEST,
        )
        own_total = own_total + partner_2(routed, "ctx", spread_bit)
    attended_out = attended.reshape(tok_rows, width).astype(jnp.bfloat16)
    grad_queries = grad_query.reshape(tok_rows, width).astype(jnp.bfloat16)
    grad_keys = own_total[0].reshape(tok_rows, width).astype(jnp.bfloat16)
    grad_values = own_total[1].reshape(tok_rows, width).astype(jnp.bfloat16)
    return (attended_out, grad_queries, grad_keys, grad_values)


def solution(mesh):
    placed = (
        P(("dp", "ctx"), None),
        P(("dp", "ctx"), None),
        P(("dp", "ctx"), None),
        P(("dp", "ctx"), None),
        P(("dp", "ctx"), None),
        P("dp"),
    )
    return jax.shard_map(
        local,
        mesh=mesh,
        in_specs=placed,
        out_specs=(
            P(("dp", "ctx"), None),
            P(("dp", "ctx"), None),
            P(("dp", "ctx"), None),
            P(("dp", "ctx"), None),
        ),
        check_vma=False,
    )
```

profile of v0, /device:TPU:96, one launch (start us, length us, event | category | flops | bytes accessed | tf_op | source)
XLA Modules:
  0.0 459.5 jit_solution(9011491721710918860)
XLA Ops:
  9.2 3.2 collective-permute-start.4
  20.5 5.8 %collective-permute-start.1 = (bf16[2,64,1024]{2,1,0:T(8,128)(2,1)S(1)}, bf16[2,64,1024]{2,1,0:T(8,128)(2,1)S(1)}, u32[]{:S(2)}, u32[]{:S(2)}) collective-permute-start(bf16[2,64,1024]{2,1,0:T(8,128)(2,1)S(1)} %get-tuple-element.48), channel_id=1, source_target_pairs={{1,0},{2,1},{3,2},{4,3},{5,4},{6,5},{7,6},{8,7},{9,8},{10,9},{11,1... | collective-permute-start | bytes 786440 | tf_op jit(solution)/shard_map/ppermute | solution.py:22
  31.1 9.4 %collective-permute-done = bf16[2,64,1024]{2,1,0:T(8,128)(2,1)S(1)} collective-permute-done((bf16[2,64,1024]{2,1,0:T(8,128)(2,1)S(1)}, bf16[2,64,1024]{2,1,0:T(8,128)(2,1)S(1)}, u32[]{:S(2)}, u32[]{:S(2)}) %collective-permute-start) | collective-permute-done | bytes 262176 | tf_op jit(solution)/shard_map/ppermute | solution.py:21
  44.1 2.6 fusion.15
  49.0 2.6 fusion.13
  53.9 2.6 fusion.14
  58.8 234.1 %all-reduce.6.cloned.1.call-done = (bf16[2,1,64,1024]{3,2,1,0:T(8,128)(2,1)}, bf16[2,1,64,1024]{3,2,0,1:T(8,128)(2,1)}) async-done(((bf16[2,1,64,1024]{3,2,1,0:T(8,128)(2,1)}, bf16[2,1,64,1024]{3,2,0,1:T(8,128)(2,1)}), (bf16[2,1,64,1024]{3,2,1,0:T(8,128)(2,1)}, bf16[2,1,64,1024]{3,2,0,1:T(8,128)(2,1)})) %all-reduce.6.cloned.1.call-update) | async-done | bytes 524304 | tf_op jit(solution)/shard_map/psum | solution.py:29
  299.1 10.3 %concatenate.15 = bf16[2,2,512,1024]{2,3,1,0:T(8,128)(2,1)} concatenate(bf16[2,2,64,1024]{2,3,1,0:T(8,128)(2,1)S(1)} %copy.75, bf16[2,2,64,1024]{2,3,1,0:T(8,128)(2,1)S(1)} %copy.76, bf16[2,2,64,1024]{2,3,1,0:T(8,128)(2,1)S(1)} %copy.77, bf16[2,2,128,1024]{2,3,1,0:T(8,128)(2,1)} %broadcast_in_dim.25, bf16[2,2,64,1024]{2,3,1,0:T(8,128)(2,1)} %copy.42, ...), dimensions={2} | concatenate | bytes 8388608 | tf_op jit(solution)/shard_map/concatenate | solution.py:116
  309.4 4.0 fusion.51
  313.4 3.4 fusion.57
  316.8 5.0 %convolution_bitcast_fusion = f32[2,512,16,64]{1,3,2,0:T(8,128)} fusion(bf16[2,64,16,64]{1,3,2,0:T(8,128)(2,1)S(1)} %copy-done.10, f32[2,16,64,512]{3,2,1,0:T(8,128)} %get-tuple-element.57, f32[2,16,64]{2,1,0:T(8,128)S(1)} %get-tuple-element.56), kind=kOutput, calls=%fused_computation.11 | convolution fusion | flops 136314880 | bytes 8658944 | tf_op jit(solution)/shard_map/jhqk,jqhd->jkhd/dot_general | solution.py:68
  324.1 2.6 convolution_bitcast_fusion.1
  326.8 7.1 %reshape.141 = f32[1,2,8,64,1024]{3,2,4,1,0:T(8,128)} reshape(f32[2,512,16,64]{1,3,2,0:T(8,128)} %convolution_bitcast_fusion.1) | data formatting | bytes 8388608 | tf_op jit(solution)/shard_map/stack | solution.py:137
  333.8 8.6 %copy.53 = f32[1,2,8,64,1024]{4,1,3,0,2:T(2,128)} copy(f32[1,2,8,64,1024]{3,2,4,1,0:T(8,128)} %reshape.141) | data formatting | bytes 8388608 | tf_op jit(solution)/shard_map/stack | solution.py:137
  342.5 7.1 %reshape.142 = f32[1,2,8,64,1024]{3,2,4,1,0:T(8,128)} reshape(f32[2,512,16,64]{1,3,2,0:T(8,128)} %convolution_bitcast_fusion) | data formatting | bytes 8388608 | tf_op jit(solution)/shard_map/stack | solution.py:137
  349.6 8.6 %copy.54 = f32[1,2,8,64,1024]{4,1,3,0,2:T(2,128)} copy(f32[1,2,8,64,1024]{3,2,4,1,0:T(8,128)} %reshape.142) | data formatting | bytes 8388608 | tf_op jit(solution)/shard_map/stack | solution.py:137
  358.2 3.6 fusion.20
  362.0 2.3 fusion.19
  364.3 2.3 fusion.21
  378.4 8.8 %collective-permute-start.9 = (f32[2,2,64,1024]{3,2,0,1:T(8,128)}, f32[2,2,64,1024]{3,2,0,1:T(8,128)}, u32[]{:S(2)}, u32[]{:S(2)}) collective-permute-start(f32[2,2,64,1024]{3,2,0,1:T(8,128)} %bitcast.128), channel_id=1, source_target_pairs={{0,4},{1,5},{2,6},{3,7},{4,0},{5,1},{6,2},{7,3},{8,12},{9,13},{10,... | collective-permute-start | bytes 3145736 | tf_op jit(solution)/shard_map/ppermute | solution.py:33
  387.2 5.5 %collective-permute-start.8 = (f32[2,2,64,1024]{3,2,0,1:T(8,128)}, f32[2,2,64,1024]{3,2,0,1:T(8,128)}, u32[]{:S(2)}, u32[]{:S(2)}) collective-permute-start(f32[2,2,64,1024]{3,2,0,1:T(8,128)} %bitcast.129), channel_id=1, source_target_pairs={{0,8},{1,9},{2,10},{3,11},{4,12},{5,13},{6,14},{7,15},{8,0},{9,1},... | collective-permute-start | bytes 3145736 | tf_op jit(solution)/shard_map/ppermute | solution.py:33
  401.3 2.5 collective-permute-start.6
  403.8 3.1 fusion.12
  411.1 37.3 %collective-permute-done.6 = f32[2,64,1024]{2,1,0:T(8,128)} collective-permute-done((f32[2,64,1024]{2,1,0:T(8,128)}, f32[2,64,1024]{2,1,0:T(8,128)}, u32[]{:S(2)}, u32[]{:S(2)}) %collective-permute-start.6) | collective-permute-done | bytes 524320 | tf_op jit(solution)/shard_map/ppermute | solution.py:39
  (90 shorter events, 60.0 us)
Async XLA Ops:
  7.2 33.4 %copy-start.6 = (bf16[128,1024]{1,0:T(8,128)(2,1)S(1)}, bf16[128,1024]{1,0:T(8,128)(2,1)}, u32[]{:S(2)}) copy-start(bf16[128,1024]{1,0:T(8,128)(2,1)} %param.12) | copy-start | bytes 786436
  7.2 33.3 %copy-start.5 = (bf16[128,1024]{1,0:T(8,128)(2,1)S(1)}, bf16[128,1024]{1,0:T(8,128)(2,1)}, u32[]{:S(2)}) copy-start(bf16[128,1024]{1,0:T(8,128)(2,1)} %param.11) | copy-start | bytes 786436
  7.2 21.9 %copy-start.11 = (bf16[128,1024]{1,0:T(8,128)(2,1)S(1)}, bf16[128,1024]{1,0:T(8,128)(2,1)}, u32[]{:S(2)}) copy-start(bf16[128,1024]{1,0:T(8,128)(2,1)} %param.13) | copy-start | bytes 786436
  7.2 23.7 %copy-start.12 = (s32[2,3]{1,0:T(2,128)S(1)}, s32[2,3]{1,0:T(2,128)}, u32[]{:S(2)}) copy-start(s32[2,3]{1,0:T(2,128)} %param.14) | copy-start | bytes 76
  7.2 285.7 %all-reduce.6.cloned.1.call-start = ((), (), s32[]{:S(2)}) async-start(), calls=%async_computation | async-start | bytes 1048576 | tf_op jit(solution)/shard_map/psum | solution.py:29
  9.2 34.9 %collective-permute-start.4 = (bf16[2,128,1024]{2,1,0:T(8,128)(2,1)}, bf16[2,128,1024]{2,1,0:T(8,128)(2,1)}, u32[]{:S(2)}, u32[]{:S(2)}) collective-permute-start(bf16[2,128,1024]{2,1,0:T(8,128)(2,1)} %pad_maximum_fusion.2), channel_id=1, source_target_pairs={{0,4},{1,5},{2,6},{3,7},{4,0},{5,1},{6,2},{7,3},{8,12},{9,13},{10,... | collective-permute-start | bytes 1572872 | tf_op jit(solution)/shard_map/ppermute | solution.py:33
  12.4 36.6 %collective-permute-start.2 = (bf16[2,128,1024]{2,1,0:T(8,128)(2,1)}, bf16[2,128,1024]{2,1,0:T(8,128)(2,1)}, u32[]{:S(2)}, u32[]{:S(2)}) collective-permute-start(bf16[2,128,1024]{2,1,0:T(8,128)(2,1)} %pad_maximum_fusion.2), channel_id=1, source_target_pairs={{0,16},{1,17},{2,18},{3,19},{4,20},{5,21},{6,22},{7,23},{8,24},{9,... | collective-permute-start | bytes 1572872 | tf_op jit(solution)/shard_map/ppermute | solution.py:33
  12.4 41.5 %collective-permute-start.3 = (bf16[2,128,1024]{2,1,0:T(8,128)(2,1)}, bf16[2,128,1024]{2,1,0:T(8,128)(2,1)}, u32[]{:S(2)}, u32[]{:S(2)}) collective-permute-start(bf16[2,128,1024]{2,1,0:T(8,128)(2,1)} %pad_maximum_fusion.2), channel_id=1, source_target_pairs={{0,8},{1,9},{2,10},{3,11},{4,12},{5,13},{6,14},{7,15},{8,0},{9,1},... | collective-permute-start | bytes 1572872 | tf_op jit(solution)/shard_map/ppermute | solution.py:33
  18.6 21.9 %collective-permute-start = (bf16[2,64,1024]{2,1,0:T(8,128)(2,1)S(1)}, bf16[2,64,1024]{2,1,0:T(8,128)(2,1)S(1)}, u32[]{:S(2)}, u32[]{:S(2)}) collective-permute-start(bf16[2,64,1024]{2,1,0:T(8,128)(2,1)S(1)} %get-tuple-element.47), channel_id=1, source_target_pairs={{0,1},{1,2},{2,3},{3,4},{4,5},{5,6},{6,7},{7,8},{8,9},{9,10},{10,1... | collective-permute-start | bytes 786440 | tf_op jit(solution)/shard_map/ppermute | solution.py:21
  20.5 20.0 %collective-permute-start.1 = (bf16[2,64,1024]{2,1,0:T(8,128)(2,1)S(1)}, bf16[2,64,1024]{2,1,0:T(8,128)(2,1)S(1)}, u32[]{:S(2)}, u32[]{:S(2)}) collective-permute-start(bf16[2,64,1024]{2,1,0:T(8,128)(2,1)S(1)} %get-tuple-element.48), channel_id=1, source_target_pairs={{1,0},{2,1},{3,2},{4,3},{5,4},{6,5},{7,6},{8,7},{9,8},{10,9},{11,1... | collective-permute-start | bytes 786440 | tf_op jit(solution)/shard_map/ppermute | solution.py:22
  309.4 4.0 copy-start.9
  313.4 8.4 %copy-start.2 = (bf16[1,2,512,1024]{2,3,1,0:T(8,128)(2,1)}, bf16[1,2,512,1024]{2,3,1,0:T(8,128)(2,1)S(1)}, u32[]{:S(2)}) copy-start(bf16[1,2,512,1024]{2,3,1,0:T(8,128)(2,1)S(1)} %get-tuple-element.36) | copy-start | bytes 6291460
  313.4 3.4 copy-start.10
  316.8 5.0 %copy-start.3 = (f32[2,16,64,512]{3,2,1,0:T(8,128)S(1)}, f32[2,16,64,512]{3,2,1,0:T(8,128)}, u32[]{:S(2)}) copy-start(f32[2,16,64,512]{3,2,1,0:T(8,128)} %get-tuple-element.57) | copy-start | bytes 12582916
  316.8 5.0 %copy-start.7 = (bf16[1,2,512,1024]{2,3,1,0:T(8,128)(2,1)S(1)}, bf16[1,2,512,1024]{2,3,1,0:T(8,128)(2,1)}, u32[]{:S(2)}) copy-start(bf16[1,2,512,1024]{2,3,1,0:T(8,128)(2,1)} %get-tuple-element.37) | copy-start | bytes 6291460
  358.2 3.6 copy-start
  358.2 3.8 copy-start.1
  372.2 20.6 %copy-start.4 = (f32[2,16,64,512]{3,2,1,0:T(8,128)S(1)}, f32[2,16,64,512]{3,2,1,0:T(8,128)}, u32[]{:S(2)}) copy-start(f32[2,16,64,512]{3,2,1,0:T(8,128)} %get-tuple-element.57) | copy-start | bytes 12582916
  372.2 20.6 %copy-start.8 = (bf16[1,2,512,1024]{2,3,1,0:T(8,128)(2,1)S(1)}, bf16[1,2,512,1024]{2,3,1,0:T(8,128)(2,1)}, u32[]{:S(2)}) copy-start(bf16[1,2,512,1024]{2,3,1,0:T(8,128)(2,1)} %get-tuple-element.37) | copy-start | bytes 6291460
  376.5 33.3 %collective-permute-start.5 = (f32[2,64,1024]{2,1,0:T(8,128)}, f32[2,64,1024]{2,1,0:T(8,128)}, u32[]{:S(2)}, u32[]{:S(2)}) collective-permute-start(f32[2,64,1024]{2,1,0:T(8,128)} %bitcast.131), channel_id=1, source_target_pairs={{1,0},{2,1},{3,2},{4,3},{5,4},{6,5},{7,6},{8,7},{9,8},{10,9},{11,1... | collective-permute-start | bytes 1572872 | tf_op jit(solution)/shard_map/ppermute | solution.py:39
  378.4 71.1 %collective-permute-start.9 = (f32[2,2,64,1024]{3,2,0,1:T(8,128)}, f32[2,2,64,1024]{3,2,0,1:T(8,128)}, u32[]{:S(2)}, u32[]{:S(2)}) collective-permute-start(f32[2,2,64,1024]{3,2,0,1:T(8,128)} %bitcast.128), channel_id=1, source_target_pairs={{0,4},{1,5},{2,6},{3,7},{4,0},{5,1},{6,2},{7,3},{8,12},{9,13},{10,... | collective-permute-start | bytes 3145736 | tf_op jit(solution)/shard_map/ppermute | solution.py:33
  387.2 62.3 %collective-permute-start.7 = (f32[2,2,64,1024]{3,2,0,1:T(8,128)}, f32[2,2,64,1024]{3,2,0,1:T(8,128)}, u32[]{:S(2)}, u32[]{:S(2)}) collective-permute-start(f32[2,2,64,1024]{3,2,0,1:T(8,128)} %bitcast.130), channel_id=1, source_target_pairs={{0,16},{1,17},{2,18},{3,19},{4,20},{5,21},{6,22},{7,23},{8,24},{9,... | collective-permute-start | bytes 3145736 | tf_op jit(solution)/shard_map/ppermute | solution.py:33
  387.2 62.3 %collective-permute-start.8 = (f32[2,2,64,1024]{3,2,0,1:T(8,128)}, f32[2,2,64,1024]{3,2,0,1:T(8,128)}, u32[]{:S(2)}, u32[]{:S(2)}) collective-permute-start(f32[2,2,64,1024]{3,2,0,1:T(8,128)} %bitcast.129), channel_id=1, source_target_pairs={{0,8},{1,9},{2,10},{3,11},{4,12},{5,13},{6,14},{7,15},{8,0},{9,1},... | collective-permute-start | bytes 3145736 | tf_op jit(solution)/shard_map/ppermute | solution.py:33
  401.3 47.0 %collective-permute-start.6 = (f32[2,64,1024]{2,1,0:T(8,128)}, f32[2,64,1024]{2,1,0:T(8,128)}, u32[]{:S(2)}, u32[]{:S(2)}) collective-permute-start(f32[2,64,1024]{2,1,0:T(8,128)} %bitcast.132), channel_id=1, source_target_pairs={{0,1},{1,2},{2,3},{3,4},{4,5},{5,6},{6,7},{7,8},{8,9},{9,10},{10,1... | collective-permute-start | bytes 1572872 | tf_op jit(solution)/shard_map/ppermute | solution.py:39
Sparse Core Ops, SparseCore 0:
  26.4 266.4 all-reduce.5
where the time goes:
time: 461 us; the launch traced here: 459 us
  waiting for transfers between devices  281 us (61%)
  local copies, waits for them, and re-layouts  83.4 us (18%)
  matrix products  33.1 us (7%)
  starting transfers between devices  29.7 us (6%)
  between operations  16.9 us (4%)
  other arithmetic  15.4 us (3%)
    psum x1, waiting for transfers between devices, from_root(): return lax.psum(block, axis)  234 us
    ppermute x2, waiting for transfers between devices, passed_along(): return lax.ppermute(array, axis, pairs)  37.3 us
    another operation x4, local copies, waits for them, and re-layouts, local(): jnp.stack([grad_key, grad_value])  31.5 us
    ppermute x6, starting transfers between devices, partner_2(): lax.ppermute(array, axis, [(i, i ^ 1 << distance) for i in range(lax.axis...  17.7 us
    concatenate x1, local copies, waits for them, and re-layouts, local(): every_key = jnp.concatenate([window, global_part] + random_parts, axis=2)  10.3 us
    ppermute x1, waiting for transfers between devices, padded_2(): before = lax.ppermute(last, axis, up)  9.38 us
  transfers between devices with their start and end apart: 11, of which 3 were waited for; matrix products, arithmetic and copies ran while one was open for 9% of the time, Pallas kernels for 0%

commit v1 on v0

--- a/solution.py
+++ b/solution.py
@@ -26,7 +26,7 @@
 
 def from_root(block, axis, source):
     block = jnp.where(lax.axis_index(axis) == source, block, jnp.zeros_like(block))
-    return lax.psum(block, axis)
+    return jnp.sum(lax.all_gather(block, axis), axis=0)
 
 
 def partner_2(array, axis, distance):

time: 461 us -> 338 us (0.73)
  the two profiles are of different devices: /device:TPU:96 before, /device:TPU:36 now
where the time goes in v1:
time: 338 us; the launch traced here: 331 us
  waiting for transfers between devices  146 us (43%)
  local copies, waits for them, and re-layouts  84.7 us (25%)
  matrix products  33.2 us (10%)
  other arithmetic  26.7 us (8%)
  starting transfers between devices  23.8 us (7%)
  between operations  17.2 us (5%)
    all_gather x2, waiting for transfers between devices, from_root(): return jnp.sum(lax.all_gather(block, axis), axis=0)  85.2 us
    ppermute x2, waiting for transfers between devices, passed_along(): return lax.ppermute(array, axis, pairs)  34.1 us
    another operation x4, local copies, waits for them, and re-layouts, local(): jnp.stack([grad_key, grad_value])  31.6 us
    ppermute x1, waiting for transfers between devices, padded_2(): before = lax.ppermute(last, axis, up)  25.8 us
    reduce_sum x2, other arithmetic, from_root(): return jnp.sum(lax.all_gather(block, axis), axis=0)  11.9 us
    concatenate x1, local copies, waits for them, and re-layouts, local(): every_key = jnp.concatenate([window, global_part] + random_parts, axis=2)  10.3 us
    ppermute x6, starting transfers between devices, partner_2(): lax.ppermute(array, axis, [(i, i ^ 1 << distance) for i in range(lax.axis...  10.1 us
    dot_general x3, matrix products, local(): jnp.einsum('jb,sjqd->sbqd', pickers[matching].astype(jnp.float32), terms,...  8.28 us
  transfers between devices with their start and end apart: 12, of which 4 were waited for; matrix products, arithmetic and copies ran while one was open for 14% of the time, Pallas kernels for 0%

profile of v1, /device:TPU:36, one launch (start us, length us, event | category | flops | bytes accessed | tf_op | source)
XLA Modules:
  0.0 331.3 jit_solution(13053201926568808768)
XLA Ops:
  16.1 3.2 collective-permute-start.4
  19.3 3.3 collective-permute-start.2
  24.6 5.8 %collective-permute-start.1 = (bf16[2,64,1024]{2,1,0:T(8,128)(2,1)S(1)}, bf16[2,64,1024]{2,1,0:T(8,128)(2,1)S(1)}, u32[]{:S(2)}, u32[]{:S(2)}) collective-permute-start(bf16[2,64,1024]{2,1,0:T(8,128)(2,1)S(1)} %get-tuple-element.46), channel_id=1, source_target_pairs={{1,0},{2,1},{3,2},{4,3},{5,4},{6,5},{7,6},{8,7},{9,8},{10,9},{11,1... | collective-permute-start | bytes 786440 | tf_op jit(solution)/shard_map/ppermute | solution.py:22
  35.1 25.8 %collective-permute-done = bf16[2,64,1024]{2,1,0:T(8,128)(2,1)S(1)} collective-permute-done((bf16[2,64,1024]{2,1,0:T(8,128)(2,1)S(1)}, bf16[2,64,1024]{2,1,0:T(8,128)(2,1)S(1)}, u32[]{:S(2)}, u32[]{:S(2)}) %collective-permute-start) | collective-permute-done | bytes 262176 | tf_op jit(solution)/shard_map/ppermute | solution.py:21
  64.5 2.6 fusion.15
  67.1 2.7 copy.74
  74.8 2.6 fusion.14
  79.7 19.3 %all-gather.5.cloned.1.call-done = bf16[64,64,1024]{2,1,0:T(8,128)(2,1)} async-done(((bf16[2,64,1024]{2,1,0:T(8,128)(2,1)}), bf16[64,64,1024]{2,1,0:T(8,128)(2,1)}) %all-gather.5.cloned.1.call-update) | async-done | bytes 8388624 | tf_op jit(solution)/shard_map/all_gather | solution.py:29
  99.0 5.6 %reduce_sum.42 = bf16[2,64,1024]{2,1,0:T(8,128)(2,1)S(1)} reduce(bf16[32,2,64,1024]{3,2,1,0:T(8,128)(2,1)} %bitcast.132, bf16[]{:T(256)} %constant.102.clone.1), dimensions={0}, to_apply=%region_0.1 | reduce | flops 4063232 | bytes 8650754 | tf_op jit(solution)/shard_map/reduce_sum | solution.py:29
  104.5 65.9 %all-gather.7.cloned.1.call-done = bf16[64,64,1024]{2,1,0:T(8,128)(2,1)} async-done(((bf16[2,64,1024]{2,1,0:T(8,128)(2,1)}), bf16[64,64,1024]{2,1,0:T(8,128)(2,1)}) %all-gather.7.cloned.1.call-update) | async-done | bytes 8388624 | tf_op jit(solution)/shard_map/all_gather | solution.py:29
  170.4 6.3 %reduce_sum.43 = bf16[2,64,1024]{2,1,0:T(8,128)(2,1)} reduce(bf16[32,2,64,1024]{3,2,1,0:T(8,128)(2,1)} %bitcast.133, bf16[]{:T(256)} %constant.102.clone.1), dimensions={0}, to_apply=%region_1.2 | reduce | flops 4063232 | bytes 8650754 | tf_op jit(solution)/shard_map/reduce_sum | solution.py:29
  182.8 10.3 %concatenate.15 = bf16[2,2,512,1024]{2,3,1,0:T(8,128)(2,1)} concatenate(bf16[2,2,64,1024]{2,3,1,0:T(8,128)(2,1)S(1)} %copy.105, bf16[2,2,64,1024]{2,3,1,0:T(8,128)(2,1)S(1)} %copy.106, bf16[2,2,64,1024]{2,3,1,0:T(8,128)(2,1)S(1)} %copy.107, bf16[2,2,128,1024]{2,3,1,0:T(8,128)(2,1)} %broadcast_in_dim.25, bf16[2,2,64,1024]{2,3,1,0:T(8,128)(2,1)} %copy.72, ...), dimensions={2} | concatenate | bytes 8388608 | tf_op jit(solution)/shard_map/concatenate | solution.py:116
  193.1 4.0 %fusion.49 = (bf16[1,2,512,1024]{2,3,1,0:T(8,128)(2,1)S(1)}, bf16[1,2,512,1024]{2,3,1,0:T(8,128)(2,1)}) fusion(bf16[2,2,512,1024]{2,3,1,0:T(8,128)(2,1)} %concatenate.15), kind=kLoop, calls=%fused_computation.97 | loop fusion | bytes 8388608 | tf_op jit(solution)/shard_map/slice | solution.py:117
  197.1 3.4 %fusion.55 = (f32[2,16,64]{2,1,0:T(8,128)S(1)}, f32[2,16,64,512]{3,2,1,0:T(8,128)}) fusion(pred[2,512]{1,0:T(4,128)(4,1)S(1)} %add_add_fusion, bf16[2,64,16,64]{1,3,2,0:T(8,128)(2,1)S(1)} %copy-done.9, bf16[2,512,16,64]{1,3,2,0:T(8,128)(2,1)S(1)} %bitcast.134), kind=kOutput, calls=%fused_computation.103 | convolution fusion | flops 138412544 | bytes 6562816 | tf_op jit(solution)/shard_map/sub | solution.py:50
  200.5 5.0 %convolution_bitcast_fusion = f32[2,512,16,64]{1,3,2,0:T(8,128)} fusion(bf16[2,64,16,64]{1,3,2,0:T(8,128)(2,1)S(1)} %copy-done.10, f32[2,16,64,512]{3,2,1,0:T(8,128)} %get-tuple-element.55, f32[2,16,64]{2,1,0:T(8,128)S(1)} %get-tuple-element.54), kind=kOutput, calls=%fused_computation.11 | convolution fusion | flops 136314880 | bytes 8658944 | tf_op jit(solution)/shard_map/jhqk,jqhd->jkhd/dot_general | solution.py:68
  207.8 2.6 convolution_bitcast_fusion.1
  210.4 7.1 %reshape.143 = f32[1,2,8,64,1024]{3,2,4,1,0:T(8,128)} reshape(f32[2,512,16,64]{1,3,2,0:T(8,128)} %convolution_bitcast_fusion.1) | data formatting | bytes 8388608 | tf_op jit(solution)/shard_map/stack | solution.py:137
  217.5 8.8 %copy.83 = f32[1,2,8,64,1024]{4,1,3,0,2:T(2,128)} copy(f32[1,2,8,64,1024]{3,2,4,1,0:T(8,128)} %reshape.143) | data formatting | bytes 8388608 | tf_op jit(solution)/shard_map/stack | solution.py:137
  226.3 7.1 %reshape.144 = f32[1,2,8,64,1024]{3,2,4,1,0:T(8,128)} reshape(f32[2,512,16,64]{1,3,2,0:T(8,128)} %convolution_bitcast_fusion) | data formatting | bytes 8388608 | tf_op jit(solution)/shard_map/stack | solution.py:137
  233.4 8.6 %copy.84 = f32[1,2,8,64,1024]{4,1,3,0,2:T(2,128)} copy(f32[1,2,8,64,1024]{3,2,4,1,0:T(8,128)} %reshape.144) | data formatting | bytes 8388608 | tf_op jit(solution)/shard_map/stack | solution.py:137
  242.0 3.6 %fusion.20 = f32[2,64,1024,2]{2,3,1,0:T(2,128)S(1)} fusion(f32[1,2,8,64,1024]{4,1,3,0,2:T(2,128)} %copy.84, f32[1,2,8,64,1024]{4,1,3,0,2:T(2,128)} %copy.83, s32[2]{0:T(128)S(1)} %get-tuple-element.30), kind=kOutput, calls=%fused_computation.43 | convolution fusion | flops 6553604 | bytes 9437192 | tf_op jit(solution)/shard_map/jb,sjqd->sbqd/dot_general | solution.py:151
  260.5 4.0 %collective-permute-start.5 = (f32[2,64,1024]{2,1,0:T(8,128)}, f32[2,64,1024]{2,1,0:T(8,128)}, u32[]{:S(2)}, u32[]{:S(2)}) collective-permute-start(f32[2,64,1024]{2,1,0:T(8,128)} %bitcast.130), channel_id=1, source_target_pairs={{1,0},{2,1},{3,2},{4,3},{5,4},{6,5},{7,6},{8,7},{9,8},{10,9},{11,1... | collective-permute-start | bytes 1572872 | tf_op jit(solution)/shard_map/ppermute | solution.py:39
  278.6 3.1 fusion.12
  285.9 34.1 %collective-permute-done.6 = f32[2,64,1024]{2,1,0:T(8,128)} collective-permute-done((f32[2,64,1024]{2,1,0:T(8,128)}, f32[2,64,1024]{2,1,0:T(8,128)}, u32[]{:S(2)}, u32[]{:S(2)}) %collective-permute-start.6) | collective-permute-done | bytes 524320 | tf_op jit(solution)/shard_map/ppermute | solution.py:39
  (96 shorter events, 69.3 us)
Async XLA Ops:
  7.2 53.7 %copy-start.6 = (bf16[128,1024]{1,0:T(8,128)(2,1)S(1)}, bf16[128,1024]{1,0:T(8,128)(2,1)}, u32[]{:S(2)}) copy-start(bf16[128,1024]{1,0:T(8,128)(2,1)} %param.12) | copy-start | bytes 786436
  7.2 53.7 %copy-start.5 = (bf16[128,1024]{1,0:T(8,128)(2,1)S(1)}, bf16[128,1024]{1,0:T(8,128)(2,1)}, u32[]{:S(2)}) copy-start(bf16[128,1024]{1,0:T(8,128)(2,1)} %param.11) | copy-start | bytes 786436
  7.2 25.9 %copy-start.11 = (bf16[128,1024]{1,0:T(8,128)(2,1)S(1)}, bf16[128,1024]{1,0:T(8,128)(2,1)}, u32[]{:S(2)}) copy-start(bf16[128,1024]{1,0:T(8,128)(2,1)} %param.13) | copy-start | bytes 786436
  7.2 27.7 %copy-start.12 = (s32[2,3]{1,0:T(2,128)S(1)}, s32[2,3]{1,0:T(2,128)}, u32[]{:S(2)}) copy-start(s32[2,3]{1,0:T(2,128)} %param.14) | copy-start | bytes 76
  7.2 91.8 %all-gather.5.cloned.1.call-start = ((), (), s32[]{:S(2)}) async-start(), calls=%async_computation | async-start | bytes 8650752 | tf_op jit(solution)/shard_map/all_gather | solution.py:29
  13.4 157.0 %all-gather.7.cloned.1.call-start = ((), (), s32[]{:S(2)}) async-start(), calls=%async_computation.1 | async-start | bytes 8650752 | tf_op jit(solution)/shard_map/all_gather | solution.py:29
  16.1 48.4 %collective-permute-start.4 = (bf16[2,128,1024]{2,1,0:T(8,128)(2,1)}, bf16[2,128,1024]{2,1,0:T(8,128)(2,1)}, u32[]{:S(2)}, u32[]{:S(2)}) collective-permute-start(bf16[2,128,1024]{2,1,0:T(8,128)(2,1)} %pad_maximum_fusion.2), channel_id=1, source_target_pairs={{0,4},{1,5},{2,6},{3,7},{4,0},{5,1},{6,2},{7,3},{8,12},{9,13},{10,... | collective-permute-start | bytes 1572872 | tf_op jit(solution)/shard_map/ppermute | solution.py:33
  19.3 50.6 %collective-permute-start.2 = (bf16[2,128,1024]{2,1,0:T(8,128)(2,1)}, bf16[2,128,1024]{2,1,0:T(8,128)(2,1)}, u32[]{:S(2)}, u32[]{:S(2)}) collective-permute-start(bf16[2,128,1024]{2,1,0:T(8,128)(2,1)} %pad_maximum_fusion.2), channel_id=1, source_target_pairs={{0,16},{1,17},{2,18},{3,19},{4,20},{5,21},{6,22},{7,23},{8,24},{9,... | collective-permute-start | bytes 1572872 | tf_op jit(solution)/shard_map/ppermute | solution.py:33
  22.6 52.2 %collective-permute-start.3 = (bf16[2,128,1024]{2,1,0:T(8,128)(2,1)}, bf16[2,128,1024]{2,1,0:T(8,128)(2,1)}, u32[]{:S(2)}, u32[]{:S(2)}) collective-permute-start(bf16[2,128,1024]{2,1,0:T(8,128)(2,1)} %pad_maximum_fusion.2), channel_id=1, source_target_pairs={{0,8},{1,9},{2,10},{3,11},{4,12},{5,13},{6,14},{7,15},{8,0},{9,1},... | collective-permute-start | bytes 1572872 | tf_op jit(solution)/shard_map/ppermute | solution.py:33
  22.7 38.2 %collective-permute-start = (bf16[2,64,1024]{2,1,0:T(8,128)(2,1)S(1)}, bf16[2,64,1024]{2,1,0:T(8,128)(2,1)S(1)}, u32[]{:S(2)}, u32[]{:S(2)}) collective-permute-start(bf16[2,64,1024]{2,1,0:T(8,128)(2,1)S(1)} %get-tuple-element.45), channel_id=1, source_target_pairs={{0,1},{1,2},{2,3},{3,4},{4,5},{5,6},{6,7},{7,8},{8,9},{9,10},{10,1... | collective-permute-start | bytes 786440 | tf_op jit(solution)/shard_map/ppermute | solution.py:21
  24.6 36.3 %collective-permute-start.1 = (bf16[2,64,1024]{2,1,0:T(8,128)(2,1)S(1)}, bf16[2,64,1024]{2,1,0:T(8,128)(2,1)S(1)}, u32[]{:S(2)}, u32[]{:S(2)}) collective-permute-start(bf16[2,64,1024]{2,1,0:T(8,128)(2,1)S(1)} %get-tuple-element.46), channel_id=1, source_target_pairs={{1,0},{2,1},{3,2},{4,3},{5,4},{6,5},{7,6},{8,7},{9,8},{10,9},{11,1... | collective-permute-start | bytes 786440 | tf_op jit(solution)/shard_map/ppermute | solution.py:22
  193.1 4.0 %copy-start.9 = (bf16[2,64,16,64]{1,3,2,0:T(8,128)(2,1)S(1)}, bf16[2,64,16,64]{1,3,2,0:T(8,128)(2,1)}, u32[]{:S(2)}) copy-start(bf16[2,64,16,64]{1,3,2,0:T(8,128)(2,1)} %copy.79) | copy-start | bytes 786436
  197.1 8.4 %copy-start.2 = (bf16[1,2,512,1024]{2,3,1,0:T(8,128)(2,1)}, bf16[1,2,512,1024]{2,3,1,0:T(8,128)(2,1)S(1)}, u32[]{:S(2)}) copy-start(bf16[1,2,512,1024]{2,3,1,0:T(8,128)(2,1)S(1)} %get-tuple-element.34) | copy-start | bytes 6291460
  200.5 5.0 %copy-start.3 = (f32[2,16,64,512]{3,2,1,0:T(8,128)S(1)}, f32[2,16,64,512]{3,2,1,0:T(8,128)}, u32[]{:S(2)}) copy-start(f32[2,16,64,512]{3,2,1,0:T(8,128)} %get-tuple-element.55) | copy-start | bytes 12582916
  200.5 5.0 %copy-start.7 = (bf16[1,2,512,1024]{2,3,1,0:T(8,128)(2,1)S(1)}, bf16[1,2,512,1024]{2,3,1,0:T(8,128)(2,1)}, u32[]{:S(2)}) copy-start(bf16[1,2,512,1024]{2,3,1,0:T(8,128)(2,1)} %get-tuple-element.35) | copy-start | bytes 6291460
  242.0 3.6 %copy-start = (f32[1,2,8,64,1024]{4,1,3,0,2:T(2,128)S(1)}, f32[1,2,8,64,1024]{4,1,3,0,2:T(2,128)}, u32[]{:S(2)}) copy-start(f32[1,2,8,64,1024]{4,1,3,0,2:T(2,128)} %copy.83) | copy-start | bytes 12582916
  242.0 3.8 %copy-start.1 = (f32[1,2,8,64,1024]{4,1,3,0,2:T(2,128)S(1)}, f32[1,2,8,64,1024]{4,1,3,0,2:T(2,128)}, u32[]{:S(2)}) copy-start(f32[1,2,8,64,1024]{4,1,3,0,2:T(2,128)} %copy.84) | copy-start | bytes 12582916
  256.2 11.9 %copy-start.4 = (f32[2,16,64,512]{3,2,1,0:T(8,128)S(1)}, f32[2,16,64,512]{3,2,1,0:T(8,128)}, u32[]{:S(2)}) copy-start(f32[2,16,64,512]{3,2,1,0:T(8,128)} %get-tuple-element.55) | copy-start | bytes 12582916
  256.2 11.9 %copy-start.8 = (bf16[1,2,512,1024]{2,3,1,0:T(8,128)(2,1)S(1)}, bf16[1,2,512,1024]{2,3,1,0:T(8,128)(2,1)}, u32[]{:S(2)}) copy-start(bf16[1,2,512,1024]{2,3,1,0:T(8,128)(2,1)} %get-tuple-element.35) | copy-start | bytes 6291460
  260.5 24.0 %collective-permute-start.5 = (f32[2,64,1024]{2,1,0:T(8,128)}, f32[2,64,1024]{2,1,0:T(8,128)}, u32[]{:S(2)}, u32[]{:S(2)}) collective-permute-start(f32[2,64,1024]{2,1,0:T(8,128)} %bitcast.130), channel_id=1, source_target_pairs={{1,0},{2,1},{3,2},{4,3},{5,4},{6,5},{7,6},{8,7},{9,8},{10,9},{11,1... | collective-permute-start | bytes 1572872 | tf_op jit(solution)/shard_map/ppermute | solution.py:39
  264.5 56.7 %collective-permute-start.9 = (f32[2,2,64,1024]{3,2,0,1:T(8,128)}, f32[2,2,64,1024]{3,2,0,1:T(8,128)}, u32[]{:S(2)}, u32[]{:S(2)}) collective-permute-start(f32[2,2,64,1024]{3,2,0,1:T(8,128)} %bitcast.127), channel_id=1, source_target_pairs={{0,4},{1,5},{2,6},{3,7},{4,0},{5,1},{6,2},{7,3},{8,12},{9,13},{10,... | collective-permute-start | bytes 3145736 | tf_op jit(solution)/shard_map/ppermute | solution.py:33
  265.6 55.7 %collective-permute-start.7 = (f32[2,2,64,1024]{3,2,0,1:T(8,128)}, f32[2,2,64,1024]{3,2,0,1:T(8,128)}, u32[]{:S(2)}, u32[]{:S(2)}) collective-permute-start(f32[2,2,64,1024]{3,2,0,1:T(8,128)} %bitcast.129), channel_id=1, source_target_pairs={{0,16},{1,17},{2,18},{3,19},{4,20},{5,21},{6,22},{7,23},{8,24},{9,... | collective-permute-start | bytes 3145736 | tf_op jit(solution)/shard_map/ppermute | solution.py:33
  266.8 54.4 %collective-permute-start.8 = (f32[2,2,64,1024]{3,2,0,1:T(8,128)}, f32[2,2,64,1024]{3,2,0,1:T(8,128)}, u32[]{:S(2)}, u32[]{:S(2)}) collective-permute-start(f32[2,2,64,1024]{3,2,0,1:T(8,128)} %bitcast.128), channel_id=1, source_target_pairs={{0,8},{1,9},{2,10},{3,11},{4,12},{5,13},{6,14},{7,15},{8,0},{9,1},... | collective-permute-start | bytes 3145736 | tf_op jit(solution)/shard_map/ppermute | solution.py:33
  276.7 43.4 %collective-permute-start.6 = (f32[2,64,1024]{2,1,0:T(8,128)}, f32[2,64,1024]{2,1,0:T(8,128)}, u32[]{:S(2)}, u32[]{:S(2)}) collective-permute-start(f32[2,64,1024]{2,1,0:T(8,128)} %bitcast.131), channel_id=1, source_target_pairs={{0,1},{1,2},{2,3},{3,4},{4,5},{5,6},{6,7},{7,8},{8,9},{9,10},{10,1... | collective-permute-start | bytes 1572872 | tf_op jit(solution)/shard_map/ppermute | solution.py:39
  (1 other events, 3.4 us)
Sparse Core Ops, SparseCore 0:
  13.6 85.3 all-gather.4
  101.4 68.9 all-gather.6
